TPU v7x, 512 devices: a whole 4x4x16 slice. The times are simulated.
512 devices in a mesh: space: 16 (over z), chaos: 32 (over x, y, core).
Axes of the slice: x: 4, y: 4, z: 16, core: 2. Of those that a mesh axis runs over, the one named last changes fastest.
Arguments:
- forcing: float32 [960, 64, 128], P('chaos', 'space'), may hold values from -120 to 120
- mean_field: float32 [64, 128], P('space'), may hold values from 1 to 8
- modes: float32 [12, 64, 128], P(None, 'space'), may hold values from 0.02 to 0.05
- lengths: int32 [32], replicated, may hold values from 1 to 30, 455 in all
Outputs:
- solution: float32 [960, 64, 128], P('chaos', 'space')
- norms: float32 [3], replicated
Inputs may be any that keep to these rules, and one draw needn't show every extreme that they name: Group lengths are positive, sum to 455, and the largest is exactly 30.
All inputs are finite; a program needn't handle non-finite values.
Results may differ from a plain program's by a relative error of at most 0.0001.
Values sent between devices are 32-bit elements; how exact they have to be, the bound alone decides.
No kernel may reach another device: no remote copies, remote signals or barrier semaphores. Data moves between devices by JAX's collectives and lax.ppermute only.
A program may use at most 64 MiB of HBM per device.

v0:
```python
import math
import jax
import jax.numpy as jnp
import numpy as np
from jax import lax
from jax.sharding import PartitionSpec as P

M = 12
P_SIZE = 455
ITERS = 3
spectrum_low = 0.05
spectrum_high = 3.0


def padded(shard, sides, width):
    for axis, dim in sides:
        devices, length = (lax.axis_size(axis), shard.shape[dim])
        up = [(i, (i + 1) % devices) for i in range(devices - 1)]
        down = [(j, i) for i, j in up]
        last = lax.slice_in_dim(shard, length - width, length, axis=dim)
        first = lax.slice_in_dim(shard, 0, width, axis=dim)
        before = lax.ppermute(last, axis, up)
        after = lax.ppermute(first, axis, down)
        shard = jnp.concatenate([before, shard, after], axis=dim)
    return shard


def index_key(entry):
    return tuple((int(value) for value in entry))


def chaos_tables(terms):
    indices = [np.zeros(terms, dtype=np.int64)]
    for first in range(terms):
        entry = np.zeros(terms, dtype=np.int64)
        entry[first] += 1
        indices.append(entry)
    for first in range(terms):
        for second in range(first, terms):
            entry = np.zeros(terms, dtype=np.int64)
            entry[first] += 1
            entry[second] += 1
            indices.append(entry)
    for first in range(terms):
        for second in range(first, terms):
            for third in range(second, terms):
                entry = np.zeros(terms, dtype=np.int64)
                entry[first] += 1
                entry[second] += 1
                entry[third] += 1
                indices.append(entry)
    lookup = {}
    for number, entry in enumerate(indices):
        lookup[index_key(entry)] = number
    count = len(indices)
    upward = np.full((count, terms), count, dtype=np.int64)
    downward = np.full((count, terms), count, dtype=np.int64)
    up_coef = np.zeros((count, terms))
    down_coef = np.zeros((count, terms))
    for number, entry in enumerate(indices):
        for term in range(terms):
            if entry.sum() < 3:
                other = entry.copy()
                other[term] += 1
                upward[number, term] = lookup[index_key(other)]
                up_coef[number, term] = math.sqrt(entry[term] + 1)
            if entry[term] > 0:
                other = entry.copy()
                other[term] -= 1
                downward[number, term] = lookup[index_key(other)]
                down_coef[number, term] = math.sqrt(entry[term])
    return (
        upward.astype(np.int32),
        downward.astype(np.int32),
        up_coef.astype(np.float32),
        down_coef.astype(np.float32),
    )


def shifted(values, toward):
    blank = jnp.zeros_like(values[..., :1])
    if toward > 0:
        return jnp.concatenate([values[..., 1:], blank], axis=-1)
    return jnp.concatenate([blank, values[..., :-1]], axis=-1)


def stiffness(field_pad, tile_pad):
    center_field = field_pad[..., 1:-1, :]
    center_tile = tile_pad[..., 1:-1, :]
    result = 0.5 * (center_field + field_pad[..., :-2, :]) * (center_tile - tile_pad[..., :-2, :])
    result = result + 0.5 * (center_field + field_pad[..., 2:, :]) * (
        center_tile - tile_pad[..., 2:, :]
    )
    for toward in (1, -1):
        result = result + 0.5 * (center_field + shifted(center_field, toward)) * (
            center_tile - shifted(center_tile, toward)
        )
    return result


def diagonal_of(field_pad):
    center_field = field_pad[..., 1:-1, :]
    result = 0.5 * (center_field + field_pad[..., :-2, :])
    result = result + 0.5 * (center_field + field_pad[..., 2:, :])
    for toward in (1, -1):
        result = result + 0.5 * (center_field + shifted(center_field, toward))
    return result


def local(forcing, mean_field, modes, lengths):
    slot_cap, tile_rows, tile_cols = forcing.shape
    groups = lax.axis_size("chaos")
    slot_count = slot_cap * groups
    my_group = lax.axis_index("chaos")
    upward, downward, up_coef, down_coef = chaos_tables(M)
    group_ends = jnp.cumsum(lengths).astype(jnp.int32)
    group_starts = (group_ends - lengths).astype(jnp.int32)
    slot_index = jnp.arange(slot_cap, dtype=jnp.int32)
    live_grid = slot_index[None, :] < lengths[:, None]
    ids_grid = jnp.where(live_grid, group_starts[:, None] + slot_index[None, :], -1).astype(
        jnp.int32
    )
    all_ids = ids_grid.reshape(slot_count)
    mine = lax.dynamic_slice_in_dim(ids_grid, my_group, 1, 0)[0]
    my_live = mine >= 0
    safe_ids = jnp.clip(mine, 0, P_SIZE - 1)
    up_rows = jnp.take(jnp.asarray(upward), safe_ids, axis=0)
    down_rows = jnp.take(jnp.asarray(downward), safe_ids, axis=0)
    live_float = my_live.astype(jnp.float32)
    up_weight = jnp.take(jnp.asarray(up_coef), safe_ids, axis=0) * live_float[:, None]
    down_weight = jnp.take(jnp.asarray(down_coef), safe_ids, axis=0) * live_float[:, None]
    coupling = jnp.where(
        up_rows.T[:, :, None] == all_ids[None, None, :], up_weight.T[:, :, None], 0.0
    )
    coupling = coupling + jnp.where(
        down_rows.T[:, :, None] == all_ids[None, None, :], down_weight.T[:, :, None], 0.0
    )
    coupling = coupling.reshape(M * slot_cap, slot_count)
    raw_fields = jnp.concatenate([mean_field[None], modes], axis=0)
    raw_pad = padded(raw_fields, (("space", 1),), 1)
    fields_pad = jnp.concatenate([raw_pad[:1], raw_pad[:1] * raw_pad[1:]], axis=0)
    diagonal = diagonal_of(raw_pad[0])
    theta = (spectrum_high + spectrum_low) / 2.0
    delta = (spectrum_high - spectrum_low) / 2.0
    sigma = theta / delta
    rho = 1.0 / sigma
    residual = forcing * live_float[:, None, None]
    solution = jnp.zeros_like(residual)
    direction = residual / diagonal / theta
    norm_list = []
    for sweep_index in range(ITERS):
        solution = solution + direction
        initial = jnp.zeros((M * slot_cap, tile_rows * tile_cols), jnp.float32)
        piece = jax.tree.map(
            lambda part: lax.all_gather(part, "chaos", axis=0, tiled=True), direction
        )
        count = piece.shape[0]
        block = lax.slice_in_dim(coupling, 0, count, axis=1)
        mixed = initial + jnp.dot(
            block,
            piece.reshape(count, -1),
            precision=lax.Precision.HIGHEST,
            preferred_element_type=jnp.float32,
        )
        mixed = mixed.reshape(M, slot_cap, tile_rows, tile_cols)
        stacked = jnp.concatenate([direction[None], mixed], axis=0)
        stacked = padded(stacked, (("space", 2),), 1)
        residual = residual - jnp.sum(stiffness(fields_pad[:, None], stacked), axis=0)
        partial_value = jnp.sum(residual * residual)
        norm_list.append(jnp.sqrt(lax.psum(partial_value, ("space", "chaos"))))
        if sweep_index + 1 < ITERS:
            rho_new = 1.0 / (2.0 * sigma - rho)
            direction = rho_new * rho * direction + 2.0 * rho_new / delta * (residual / diagonal)
            rho = rho_new
    norms = jnp.stack(norm_list)
    return (solution, norms)


def solution(mesh):
    in_specs = (P("chaos", "space", None), P("space", None), P(None, "space", None), P())
    out_specs = (P("chaos", "space", None), P())
    return jax.shard_map(local, mesh=mesh, in_specs=in_specs, out_specs=out_specs, check_vma=False)
```

profile of v0, /device:TPU:1, one launch (start us, length us, event | category | flops | bytes accessed | tf_op | source)
XLA Modules:
  0.0 371.4 jit_solution(11172319493625132148)
XLA Ops:
  7.2 0.8 pad_maximum_fusion.19
  8.0 4.4 %collective-permute-start = (f32[13,1,128]{2,1,0:T(1,128)S(1)}, f32[13,1,128]{2,1,0:T(1,128)S(1)}, u32[]{:S(2)}, u32[]{:S(2)}) collective-permute-start(f32[13,1,128]{2,1,0:T(1,128)S(1)} %get-tuple-element.41), channel_id=1, source_target_pairs={{0,32},{32,64},{64,96},{96,128},{128,160},{160,192},{192,224},{224... | collective-permute-start | bytes 19976 | tf_op jit(solution)/shard_map/ppermute | solution.py:22
  12.4 1.3 collective-permute-start.1
  13.7 0.8 fusion.94
  14.5 0.7 copy.30
  16.1 0.7 add_select_fusion
  17.0 0.9 fusion.83
  17.8 0.9 fusion.91
  19.6 1.5 gather_fusion.3
  21.2 1.5 gather_fusion.2
  22.7 1.5 gather_fusion.1
  24.4 1.5 gather_fusion
  26.9 0.8 fusion.71
  27.8 57.6 %all-gather.4.cloned.1.call-done = f32[960,4,128]{2,1,0:T(4,128)} async-done(((f32[30,4,128]{2,1,0:T(4,128)}), f32[960,4,128]{2,1,0:T(4,128)}) %all-gather.4.cloned.1.call-update) | async-done | bytes 1966096 | tf_op jit(solution)/shard_map/all_gather | solution.py:155
  85.3 4.5 %fusion.4 = f32[12,30,4,128]{3,1,2,0:T(8,128)S(1)} fusion(f32[12,30]{1,0:T(8,128)S(1)} %copy.35, s32[12,30]{1,0:T(8,128)S(1)} %copy.34, f32[12,30]{1,0:T(8,128)S(1)} %copy.33, s32[960]{0:T(1024)S(1)} %select_n.56, s32[12,30]{1,0:T(8,128)S(1)} %copy.32, f32[120,8,4,128]{3,2,1,0:T(4,128)} %bitcast.120), kind=kOutput, calls=%fused_computation.29 | convolution fusion | flops 2125094400 | bytes 2712960 | tf_op jit(solution)/shard_map/dot_general | solution.py:159
  89.9 3.2 collective-permute-start.2
  93.1 1.3 collective-permute-start.3
  94.8 2.6 collective-permute-done.2
  97.4 3.8 %collective-permute-done.3 = f32[13,30,1,128]{3,1,2,0:T(8,128)S(1)} collective-permute-done((f32[13,30,1,128]{3,1,2,0:T(8,128)S(1)}, f32[13,30,1,128]{3,1,2,0:T(8,128)S(1)}, u32[]{:S(2)}, u32[]{:S(2)}) %collective-permute-start.3) | collective-permute-done | bytes 199712 | tf_op jit(solution)/shard_map/ppermute | solution.py:23
  102.9 59.5 %all-gather.6.cloned.1.call-done = f32[960,4,128]{2,1,0:T(4,128)} async-done(((f32[30,4,128]{2,1,0:T(4,128)}), f32[960,4,128]{2,1,0:T(4,128)}) %all-gather.6.cloned.1.call-update) | async-done | bytes 1966096 | tf_op jit(solution)/shard_map/all_gather | solution.py:155
  162.4 4.5 %fusion.2 = f32[12,30,4,128]{3,1,2,0:T(8,128)S(1)} fusion(f32[12,30]{1,0:T(8,128)S(1)} %copy.35, s32[12,30]{1,0:T(8,128)S(1)} %copy.34, f32[12,30]{1,0:T(8,128)S(1)} %copy.33, s32[960]{0:T(1024)S(1)} %select_n.56, s32[12,30]{1,0:T(8,128)S(1)} %copy.32, f32[120,8,4,128]{3,2,1,0:T(4,128)} %bitcast.122), kind=kOutput, calls=%fused_computation.26 | convolution fusion | flops 2125094400 | bytes 2712960 | tf_op jit(solution)/shard_map/dot_general | solution.py:159
  167.0 3.2 collective-permute-start.4
  170.2 1.3 collective-permute-start.5
  171.8 2.7 collective-permute-done.4
  174.4 3.8 %collective-permute-done.5 = f32[13,30,1,128]{3,1,2,0:T(8,128)S(1)} collective-permute-done((f32[13,30,1,128]{3,1,2,0:T(8,128)S(1)}, f32[13,30,1,128]{3,1,2,0:T(8,128)S(1)}, u32[]{:S(2)}, u32[]{:S(2)}) %collective-permute-start.5) | collective-permute-done | bytes 199712 | tf_op jit(solution)/shard_map/ppermute | solution.py:23
  180.3 59.6 %all-gather.8.cloned.1.call-done = f32[960,4,128]{2,1,0:T(4,128)} async-done(((f32[30,4,128]{2,1,0:T(4,128)}), f32[960,4,128]{2,1,0:T(4,128)}) %all-gather.8.cloned.1.call-update) | async-done | bytes 1966096 | tf_op jit(solution)/shard_map/all_gather | solution.py:155
  239.9 4.5 %fusion = f32[12,30,4,128]{3,1,2,0:T(8,128)S(1)} fusion(f32[12,30]{1,0:T(8,128)S(1)} %copy.35, s32[12,30]{1,0:T(8,128)S(1)} %copy.34, f32[12,30]{1,0:T(8,128)S(1)} %copy.33, s32[960]{0:T(1024)S(1)} %select_n.56, s32[12,30]{1,0:T(8,128)S(1)} %copy.32, f32[120,8,4,128]{3,2,1,0:T(4,128)} %bitcast.121), kind=kOutput, calls=%fused_computation.23 | convolution fusion | flops 2125094400 | bytes 2712960 | tf_op jit(solution)/shard_map/dot_general | solution.py:159
  244.4 3.2 collective-permute-start.6
  247.6 1.3 collective-permute-start.7
  249.9 2.0 collective-permute-done.6
  251.9 3.8 %collective-permute-done.7 = f32[13,30,1,128]{3,1,2,0:T(8,128)S(1)} collective-permute-done((f32[13,30,1,128]{3,1,2,0:T(8,128)S(1)}, f32[13,30,1,128]{3,1,2,0:T(8,128)S(1)}, u32[]{:S(2)}, u32[]{:S(2)}) %collective-permute-start.7) | collective-permute-done | bytes 199712 | tf_op jit(solution)/shard_map/ppermute | solution.py:23
  257.1 105.2 %all-reduce.10 = (f32[]{:T(128)}, f32[]{:T(128)}, f32[]{:T(128)}) all-reduce(f32[]{:T(128)} %get-tuple-element.11, f32[]{:T(128)} %get-tuple-element.10, f32[]{:T(128)} %get-tuple-element.32), channel_id=1, replica_groups=mesh['space'=16,'chaos'=32] {'space','chaos'}, use_global_device_ids=true, to_apply=%region_9.12 | all-reduce | flops 3 | bytes 24 | tf_op jit(solution)/shard_map/psum | solution.py:170
  (44 shorter events, 10.4 us)
Async XLA Ops:
  7.2 78.2 %all-gather.4.cloned.1.call-start = ((), (), s32[]{:S(2)}) async-start(), calls=%async_computation | async-start | bytes 2027520 | tf_op jit(solution)/shard_map/all_gather | solution.py:155
  8.0 8.8 %collective-permute-start = (f32[13,1,128]{2,1,0:T(1,128)S(1)}, f32[13,1,128]{2,1,0:T(1,128)S(1)}, u32[]{:S(2)}, u32[]{:S(2)}) collective-permute-start(f32[13,1,128]{2,1,0:T(1,128)S(1)} %get-tuple-element.41), channel_id=1, source_target_pairs={{0,32},{32,64},{64,96},{96,128},{128,160},{160,192},{192,224},{224... | collective-permute-start | bytes 19976 | tf_op jit(solution)/shard_map/ppermute | solution.py:22
  12.4 4.6 %collective-permute-start.1 = (f32[13,1,128]{2,1,0:T(1,128)S(1)}, f32[13,1,128]{2,1,0:T(1,128)S(1)}, u32[]{:S(2)}, u32[]{:S(2)}) collective-permute-start(f32[13,1,128]{2,1,0:T(1,128)S(1)} %get-tuple-element.42), channel_id=1, source_target_pairs={{32,0},{64,32},{96,64},{128,96},{160,128},{192,160},{224,192},{256... | collective-permute-start | bytes 19976 | tf_op jit(solution)/shard_map/ppermute | solution.py:23
  19.5 143.0 %all-gather.6.cloned.1.call-start = ((), (), s32[]{:S(2)}) async-start(), calls=%async_computation.1 | async-start | bytes 2027520 | tf_op jit(solution)/shard_map/all_gather | solution.py:155
  89.9 7.5 %collective-permute-start.2 = (f32[13,30,1,128]{3,1,2,0:T(8,128)S(1)}, f32[13,30,1,128]{3,1,2,0:T(8,128)S(1)}, u32[]{:S(2)}, u32[]{:S(2)}) collective-permute-start(f32[13,30,1,128]{3,1,2,0:T(8,128)S(1)} %get-tuple-element.30), channel_id=1, source_target_pairs={{0,32},{32,64},{64,96},{96,128},{128,160},{160,192},{192,224},{224... | collective-permute-start | bytes 599048 | tf_op jit(solution)/shard_map/ppermute | solution.py:22
  93.1 8.1 %collective-permute-start.3 = (f32[13,30,1,128]{3,1,2,0:T(8,128)S(1)}, f32[13,30,1,128]{3,1,2,0:T(8,128)S(1)}, u32[]{:S(2)}, u32[]{:S(2)}) collective-permute-start(f32[13,30,1,128]{3,1,2,0:T(8,128)S(1)} %get-tuple-element.31), channel_id=1, source_target_pairs={{32,0},{64,32},{96,64},{128,96},{160,128},{192,160},{224,192},{256... | collective-permute-start | bytes 599048 | tf_op jit(solution)/shard_map/ppermute | solution.py:23
  101.2 0.8 copy-start
  102.8 137.1 %all-gather.8.cloned.1.call-start = ((), (), s32[]{:S(2)}) async-start(), calls=%async_computation.2 | async-start | bytes 2027520 | tf_op jit(solution)/shard_map/all_gather | solution.py:155
  167.0 7.5 %collective-permute-start.4 = (f32[13,30,1,128]{3,1,2,0:T(8,128)S(1)}, f32[13,30,1,128]{3,1,2,0:T(8,128)S(1)}, u32[]{:S(2)}, u32[]{:S(2)}) collective-permute-start(f32[13,30,1,128]{3,1,2,0:T(8,128)S(1)} %get-tuple-element.26), channel_id=1, source_target_pairs={{0,32},{32,64},{64,96},{96,128},{128,160},{160,192},{192,224},{224... | collective-permute-start | bytes 599048 | tf_op jit(solution)/shard_map/ppermute | solution.py:22
  170.2 8.1 %collective-permute-start.5 = (f32[13,30,1,128]{3,1,2,0:T(8,128)S(1)}, f32[13,30,1,128]{3,1,2,0:T(8,128)S(1)}, u32[]{:S(2)}, u32[]{:S(2)}) collective-permute-start(f32[13,30,1,128]{3,1,2,0:T(8,128)S(1)} %get-tuple-element.27), channel_id=1, source_target_pairs={{32,0},{64,32},{96,64},{128,96},{160,128},{192,160},{224,192},{256... | collective-permute-start | bytes 599048 | tf_op jit(solution)/shard_map/ppermute | solution.py:23
  244.4 7.5 %collective-permute-start.6 = (f32[13,30,1,128]{3,1,2,0:T(8,128)S(1)}, f32[13,30,1,128]{3,1,2,0:T(8,128)S(1)}, u32[]{:S(2)}, u32[]{:S(2)}) collective-permute-start(f32[13,30,1,128]{3,1,2,0:T(8,128)S(1)} %get-tuple-element.22), channel_id=1, source_target_pairs={{0,32},{32,64},{64,96},{96,128},{128,160},{160,192},{192,224},{224... | collective-permute-start | bytes 599048 | tf_op jit(solution)/shard_map/ppermute | solution.py:22
  247.6 8.1 %collective-permute-start.7 = (f32[13,30,1,128]{3,1,2,0:T(8,128)S(1)}, f32[13,30,1,128]{3,1,2,0:T(8,128)S(1)}, u32[]{:S(2)}, u32[]{:S(2)}) collective-permute-start(f32[13,30,1,128]{3,1,2,0:T(8,128)S(1)} %get-tuple-element.23), channel_id=1, source_target_pairs={{32,0},{64,32},{96,64},{128,96},{160,128},{192,160},{224,192},{256... | collective-permute-start | bytes 599048 | tf_op jit(solution)/shard_map/ppermute | solution.py:23
Sparse Core Ops, SparseCore 0:
  19.6 65.7 all-gather.3
  102.9 59.4 all-gather.5
  180.4 59.4 all-gather.7
where the time goes:
time: 372 us; the launch traced here: 371 us
  waiting for transfers between devices  196 us (53%)
  blocking collectives  105 us (28%)
  starting transfers between devices  19.2 us (5%)
  between operations  16 us (4%)
  matrix products  13.5 us (4%)
  local copies, waits for them, and re-layouts  11 us (3%)
  other arithmetic  10.8 us (3%)
    all_gather x3, waiting for transfers between devices, local(): lax.all_gather(part, 'chaos', axis=0, tiled=True)  177 us
    psum x1, blocking collectives, local(): norm_list.append(jnp.sqrt(lax.psum(partial_value, ('space', 'chaos'))))  105 us
    ppermute x4, starting transfers between devices, padded(): before = lax.ppermute(last, axis, up)  13.9 us
    dot_general x3, matrix products, local(): jnp.dot(block, piece.reshape(count, -1), precision=lax.Precision.HIGHEST,...  13.5 us
    ppermute x4, waiting for transfers between devices, padded(): after = lax.ppermute(first, axis, down)  11.6 us
  transfers between devices with their start and end apart: 11, of which 10 were waited for; matrix products, arithmetic and copies ran while one was open for 4% of the time, Pallas kernels for 0%

commit v1 on v0

--- a/solution.py
+++ b/solution.py
@@ -152,7 +152,10 @@
         solution = solution + direction
         initial = jnp.zeros((M * slot_cap, tile_rows * tile_cols), jnp.float32)
         piece = jax.tree.map(
-            lambda part: lax.all_gather(part, "chaos", axis=0, tiled=True), direction
+            lambda part: jnp.concatenate(
+                lax.all_to_all(jnp.stack([part] * lax.axis_size("chaos")), "chaos", 0, 0), axis=0
+            ),
+            direction,
         )
         count = piece.shape[0]
         block = lax.slice_in_dim(coupling, 0, count, axis=1)

time: 372 us -> 272 us (0.73)
  waiting for transfers between devices: 196 us -> 44.4 us
  blocking collectives: 105 us -> 167 us
  between operations: 16 us -> 2.96 us
  starting transfers between devices: 19.2 us -> 31.5 us
  matrix products: 13.5 us -> 8.87 us
    all_gather x3 -> x0, waiting for transfers between devices: 177 us -> none  [local(): lax.all_gather(part, 'chaos', axis=0, tiled=True)]
    all_to_all x0 -> x2, blocking collectives: none -> 62.5 us  [local(): lax.all_to_all(jnp.stack([part] * lax.axis_size('chaos')), 'chaos', 0, 0)]
    all_to_all x0 -> x1, waiting for transfers between devices: none -> 23.8 us  [local(): lax.all_to_all(jnp.stack([part] * lax.axis_size('chaos')), 'chaos', 0, 0)]
    all_to_all x0 -> x1, starting transfers between devices: none -> 9.14 us  [local(): lax.all_to_all(jnp.stack([part] * lax.axis_size('chaos')), 'chaos', 0, 0)]
    dot_general x3, matrix products: 13.5 us -> 8.87 us  [local(): jnp.dot(block, piece.reshape(count, -1), precision=lax.Precision.HIGHEST,...]
  transfers between devices with their start and end apart: 11 -> 9, of which waited for: 10 -> 8; matrix products, arithmetic and copies ran while one was open for 4% -> 3% of each run, Pallas kernels for 0% -> 0%
where the time goes in v1:
time: 272 us; the launch traced here: 271 us
  blocking collectives  167 us (61%)
  waiting for transfers between devices  44.4 us (16%)
  starting transfers between devices  31.5 us (12%)
  other arithmetic  9.34 us (3%)
  matrix products  8.87 us (3%)
  local copies, waits for them, and re-layouts  7.51 us (3%)
  between operations  2.96 us (1%)
    psum x1, blocking collectives, local(): norm_list.append(jnp.sqrt(lax.psum(partial_value, ('space', 'chaos'))))  104 us
    all_to_all x2, blocking collectives, local(): lax.all_to_all(jnp.stack([part] * lax.axis_size('chaos')), 'chaos', 0, 0)  62.5 us
    all_to_all x1, waiting for transfers between devices, local(): lax.all_to_all(jnp.stack([part] * lax.axis_size('chaos')), 'chaos', 0, 0)  23.8 us
    ppermute x4, starting transfers between devices, padded(): before = lax.ppermute(last, axis, up)  17.2 us
    ppermute x4, waiting for transfers between devices, padded(): after = lax.ppermute(first, axis, down)  13.2 us
    all_to_all x1, starting transfers between devices, local(): lax.all_to_all(jnp.stack([part] * lax.axis_size('chaos')), 'chaos', 0, 0)  9.14 us
    dot_general x3, matrix products, local(): jnp.dot(block, piece.reshape(count, -1), precision=lax.Precision.HIGHEST,...  8.87 us
    ppermute x4, waiting for transfers between devices, padded(): before = lax.ppermute(last, axis, up)  7.36 us
  transfers between devices with their start and end apart: 9, of which 8 were waited for; matrix products, arithmetic and copies ran while one was open for 3% of the time, Pallas kernels for 0%

profile of v1, /device:TPU:1, one launch (start us, length us, event | category | flops | bytes accessed | tf_op | source)
XLA Modules:
  0.0 271.5 jit_solution(11982641661533638281)
XLA Ops:
  0.6 0.8 pad_maximum_fusion.19
  1.5 4.4 %collective-permute-start = (f32[13,1,128]{2,1,0:T(1,128)S(1)}, f32[13,1,128]{2,1,0:T(1,128)S(1)}, u32[]{:S(2)}, u32[]{:S(2)}) collective-permute-start(f32[13,1,128]{2,1,0:T(1,128)S(1)} %get-tuple-element.39), channel_id=1, source_target_pairs={{0,32},{32,64},{64,96},{96,128},{128,160},{160,192},{192,224},{224... | collective-permute-start | bytes 19976 | tf_op jit(solution)/shard_map/ppermute | solution.py:22
  5.8 1.3 collective-permute-start.1
  7.1 0.8 fusion.94
  8.0 0.7 copy.20
  9.5 0.7 add_select_fusion
  10.4 0.9 fusion.83
  11.3 0.9 fusion.91
  12.2 1.6 stack.14
  13.8 9.1 %all-to-all-start = ((f32[32,30,4,128]{3,2,1,0:T(4,128)}), f32[32,30,4,128]{3,2,1,0:T(4,128)S(1)}, u32[]{:S(2)}, u32[]{:S(2)}) async-start(f32[32,30,4,128]{3,2,1,0:T(4,128)} %stack.14), calls=%async_computation | async-start | bytes 3932160 | tf_op jit(solution)/shard_map/all_to_all | solution.py:156
  26.1 23.8 %all-to-all-done = f32[32,30,4,128]{3,2,1,0:T(4,128)S(1)} async-done(((f32[32,30,4,128]{3,2,1,0:T(4,128)}), f32[32,30,4,128]{3,2,1,0:T(4,128)S(1)}, u32[]{:S(2)}, u32[]{:S(2)}) %all-to-all-start) | async-done | bytes 1966112 | tf_op jit(solution)/shard_map/all_to_all | solution.py:156
  49.9 3.0 %fusion.4 = f32[12,30,4,128]{3,1,2,0:T(8,128)S(1)} fusion(f32[12,30]{1,0:T(8,128)S(1)} %copy.25, s32[12,30]{1,0:T(8,128)S(1)} %copy.24, f32[12,30]{1,0:T(8,128)S(1)} %copy.23, s32[960]{0:T(1024)S(1)} %select_n.56, s32[12,30]{1,0:T(8,128)S(1)} %copy.22, f32[120,8,4,128]{3,2,1,0:T(4,128)S(1)} %bitcast.114), kind=kOutput, calls=%fused_computation.29 | convolution fusion | flops 2125094400 | bytes 2712960 | tf_op jit(solution)/shard_map/dot_general | solution.py:162
  52.9 3.6 %collective-permute-start.2 = (f32[13,30,1,128]{3,1,2,0:T(8,128)S(1)}, f32[13,30,1,128]{3,1,2,0:T(8,128)S(1)}, u32[]{:S(2)}, u32[]{:S(2)}) collective-permute-start(f32[13,30,1,128]{3,1,2,0:T(8,128)S(1)} %get-tuple-element.28), channel_id=1, source_target_pairs={{0,32},{32,64},{64,96},{96,128},{128,160},{160,192},{192,224},{224... | collective-permute-start | bytes 599048 | tf_op jit(solution)/shard_map/ppermute | solution.py:22
  56.5 1.3 collective-permute-start.3
  58.2 2.1 collective-permute-done.2
  60.3 5.4 %collective-permute-done.3 = f32[13,30,1,128]{3,1,2,0:T(8,128)S(1)} collective-permute-done((f32[13,30,1,128]{3,1,2,0:T(8,128)S(1)}, f32[13,30,1,128]{3,1,2,0:T(8,128)S(1)}, u32[]{:S(2)}, u32[]{:S(2)}) %collective-permute-start.3) | collective-permute-done | bytes 199712 | tf_op jit(solution)/shard_map/ppermute | solution.py:23
  66.9 31.3 %all_to_all.15 = f32[32,30,4,128]{3,2,1,0:T(4,128)S(1)} all-to-all(f32[32,30,4,128]{3,2,1,0:T(4,128)S(1)} %stack.15), channel_id=1, replica_groups=mesh['space'=16,'chaos'=32] {'chaos'}, dimensions={0} | all-to-all | bytes 3932160 | tf_op jit(solution)/shard_map/all_to_all | solution.py:156
  98.3 3.0 %fusion.2 = f32[12,30,4,128]{3,1,2,0:T(8,128)S(1)} fusion(f32[12,30]{1,0:T(8,128)S(1)} %copy.25, s32[12,30]{1,0:T(8,128)S(1)} %copy.24, f32[12,30]{1,0:T(8,128)S(1)} %copy.23, s32[960]{0:T(1024)S(1)} %select_n.56, s32[12,30]{1,0:T(8,128)S(1)} %copy.22, f32[120,8,4,128]{3,2,1,0:T(4,128)S(1)} %bitcast.116), kind=kOutput, calls=%fused_computation.26 | convolution fusion | flops 2125094400 | bytes 2712960 | tf_op jit(solution)/shard_map/dot_general | solution.py:162
  101.3 4.9 %collective-permute-start.4 = (f32[13,30,1,128]{3,1,2,0:T(8,128)S(1)}, f32[13,30,1,128]{3,1,2,0:T(8,128)S(1)}, u32[]{:S(2)}, u32[]{:S(2)}) collective-permute-start(f32[13,30,1,128]{3,1,2,0:T(8,128)S(1)} %get-tuple-element.24), channel_id=1, source_target_pairs={{0,32},{32,64},{64,96},{96,128},{128,160},{160,192},{192,224},{224... | collective-permute-start | bytes 599048 | tf_op jit(solution)/shard_map/ppermute | solution.py:22
  106.2 1.3 collective-permute-start.5
  107.8 3.0 %collective-permute-done.4 = f32[13,30,1,128]{3,1,2,0:T(8,128)S(1)} collective-permute-done((f32[13,30,1,128]{3,1,2,0:T(8,128)S(1)}, f32[13,30,1,128]{3,1,2,0:T(8,128)S(1)}, u32[]{:S(2)}, u32[]{:S(2)}) %collective-permute-start.4) | collective-permute-done | bytes 199712 | tf_op jit(solution)/shard_map/ppermute | solution.py:22
  110.7 3.8 %collective-permute-done.5 = f32[13,30,1,128]{3,1,2,0:T(8,128)S(1)} collective-permute-done((f32[13,30,1,128]{3,1,2,0:T(8,128)S(1)}, f32[13,30,1,128]{3,1,2,0:T(8,128)S(1)}, u32[]{:S(2)}, u32[]{:S(2)}) %collective-permute-start.5) | collective-permute-done | bytes 199712 | tf_op jit(solution)/shard_map/ppermute | solution.py:23
  115.2 0.7 add_add_fusion
  116.2 31.2 %all_to_all.16 = f32[32,30,4,128]{3,2,1,0:T(4,128)S(1)} all-to-all(f32[32,30,4,128]{3,2,1,0:T(4,128)S(1)} %stack.18), channel_id=1, replica_groups=mesh['space'=16,'chaos'=32] {'chaos'}, dimensions={0} | all-to-all | bytes 3932160 | tf_op jit(solution)/shard_map/all_to_all | solution.py:156
  147.4 3.0 %fusion = f32[12,30,4,128]{3,1,2,0:T(8,128)S(1)} fusion(f32[12,30]{1,0:T(8,128)S(1)} %copy.25, s32[12,30]{1,0:T(8,128)S(1)} %copy.24, f32[12,30]{1,0:T(8,128)S(1)} %copy.23, s32[960]{0:T(1024)S(1)} %select_n.56, s32[12,30]{1,0:T(8,128)S(1)} %copy.22, f32[120,8,4,128]{3,2,1,0:T(4,128)S(1)} %bitcast.115), kind=kOutput, calls=%fused_computation.23 | convolution fusion | flops 2125094400 | bytes 2712960 | tf_op jit(solution)/shard_map/dot_general | solution.py:162
  150.4 4.4 %collective-permute-start.6 = (f32[13,30,1,128]{3,1,2,0:T(8,128)S(1)}, f32[13,30,1,128]{3,1,2,0:T(8,128)S(1)}, u32[]{:S(2)}, u32[]{:S(2)}) collective-permute-start(f32[13,30,1,128]{3,1,2,0:T(8,128)S(1)} %get-tuple-element.20), channel_id=1, source_target_pairs={{0,32},{32,64},{64,96},{96,128},{128,160},{160,192},{192,224},{224... | collective-permute-start | bytes 599048 | tf_op jit(solution)/shard_map/ppermute | solution.py:22
  154.8 1.3 collective-permute-start.7
  156.1 0.7 copy.32
  157.1 2.3 collective-permute-done.6
  159.4 3.8 %collective-permute-done.7 = f32[13,30,1,128]{3,1,2,0:T(8,128)S(1)} collective-permute-done((f32[13,30,1,128]{3,1,2,0:T(8,128)S(1)}, f32[13,30,1,128]{3,1,2,0:T(8,128)S(1)}, u32[]{:S(2)}, u32[]{:S(2)}) %collective-permute-start.7) | collective-permute-done | bytes 199712 | tf_op jit(solution)/shard_map/ppermute | solution.py:23
  163.9 0.7 multiply_reduce_fusion.1
  164.5 104.4 %all-reduce.10 = (f32[]{:T(128)}, f32[]{:T(128)}, f32[]{:T(128)}) all-reduce(f32[]{:T(128)} %get-tuple-element.9, f32[]{:T(128)} %get-tuple-element.8, f32[]{:T(128)} %get-tuple-element.30), channel_id=1, replica_groups=mesh['space'=16,'chaos'=32] {'space','chaos'}, use_global_device_ids=true, to_apply=%region_9.12 | all-reduce | flops 3 | bytes 24 | tf_op jit(solution)/shard_map/psum | solution.py:173
  (54 shorter events, 8.5 us)
Async XLA Ops:
  1.5 8.8 %collective-permute-start = (f32[13,1,128]{2,1,0:T(1,128)S(1)}, f32[13,1,128]{2,1,0:T(1,128)S(1)}, u32[]{:S(2)}, u32[]{:S(2)}) collective-permute-start(f32[13,1,128]{2,1,0:T(1,128)S(1)} %get-tuple-element.39), channel_id=1, source_target_pairs={{0,32},{32,64},{64,96},{96,128},{128,160},{160,192},{192,224},{224... | collective-permute-start | bytes 19976 | tf_op jit(solution)/shard_map/ppermute | solution.py:22
  5.8 4.6 %collective-permute-start.1 = (f32[13,1,128]{2,1,0:T(1,128)S(1)}, f32[13,1,128]{2,1,0:T(1,128)S(1)}, u32[]{:S(2)}, u32[]{:S(2)}) collective-permute-start(f32[13,1,128]{2,1,0:T(1,128)S(1)} %get-tuple-element.40), channel_id=1, source_target_pairs={{32,0},{64,32},{96,64},{128,96},{160,128},{192,160},{224,192},{256... | collective-permute-start | bytes 19976 | tf_op jit(solution)/shard_map/ppermute | solution.py:23
  13.8 9.3 %copy-start.6 = (f32[455,12]{1,0:T(8,128)S(1)}, f32[455,12]{1,0:T(8,128)}, u32[]{:S(2)}) copy-start(f32[455,12]{1,0:T(8,128)} %constant.22.clone2.1) | copy-start | bytes 65524
  13.8 9.9 %copy-start.5 = (s32[455,12]{1,0:T(8,128)S(1)}, s32[455,12]{1,0:T(8,128)}, u32[]{:S(2)}) copy-start(s32[455,12]{1,0:T(8,128)} %constant.16.clone2.1) | copy-start | bytes 65524
  13.8 10.5 %copy-start.4 = (f32[455,12]{1,0:T(8,128)S(1)}, f32[455,12]{1,0:T(8,128)}, u32[]{:S(2)}) copy-start(f32[455,12]{1,0:T(8,128)} %constant.21.clone2.1) | copy-start | bytes 65524
  13.8 11.3 %copy-start.3 = (s32[455,12]{1,0:T(8,128)S(1)}, s32[455,12]{1,0:T(8,128)}, u32[]{:S(2)}) copy-start(s32[455,12]{1,0:T(8,128)} %constant.15.clone2.1) | copy-start | bytes 65524
  13.8 12.2 %copy-start.1 = (f32[12,4,128]{2,1,0:T(4,128)S(1)}, f32[12,4,128]{2,1,0:T(4,128)}, u32[]{:S(2)}) copy-start(f32[12,4,128]{2,1,0:T(4,128)} %param.14) | copy-start | bytes 73732
  13.8 12.1 %copy-start.2 = (f32[4,128]{1,0:T(4,128)S(1)}, f32[4,128]{1,0:T(4,128)}, u32[]{:S(2)}) copy-start(f32[4,128]{1,0:T(4,128)} %param.13) | copy-start | bytes 6148
  13.8 36.1 %all-to-all-start = ((f32[32,30,4,128]{3,2,1,0:T(4,128)}), f32[32,30,4,128]{3,2,1,0:T(4,128)S(1)}, u32[]{:S(2)}, u32[]{:S(2)}) async-start(f32[32,30,4,128]{3,2,1,0:T(4,128)} %stack.14), calls=%async_computation | async-start | bytes 3932160 | tf_op jit(solution)/shard_map/all_to_all | solution.py:156
  52.9 7.4 %collective-permute-start.2 = (f32[13,30,1,128]{3,1,2,0:T(8,128)S(1)}, f32[13,30,1,128]{3,1,2,0:T(8,128)S(1)}, u32[]{:S(2)}, u32[]{:S(2)}) collective-permute-start(f32[13,30,1,128]{3,1,2,0:T(8,128)S(1)} %get-tuple-element.28), channel_id=1, source_target_pairs={{0,32},{32,64},{64,96},{96,128},{128,160},{160,192},{192,224},{224... | collective-permute-start | bytes 599048 | tf_op jit(solution)/shard_map/ppermute | solution.py:22
  56.5 9.2 %collective-permute-start.3 = (f32[13,30,1,128]{3,1,2,0:T(8,128)S(1)}, f32[13,30,1,128]{3,1,2,0:T(8,128)S(1)}, u32[]{:S(2)}, u32[]{:S(2)}) collective-permute-start(f32[13,30,1,128]{3,1,2,0:T(8,128)S(1)} %get-tuple-element.29), channel_id=1, source_target_pairs={{32,0},{64,32},{96,64},{128,96},{160,128},{192,160},{224,192},{256... | collective-permute-start | bytes 599048 | tf_op jit(solution)/shard_map/ppermute | solution.py:23
  65.7 0.8 copy-start
  101.3 9.5 %collective-permute-start.4 = (f32[13,30,1,128]{3,1,2,0:T(8,128)S(1)}, f32[13,30,1,128]{3,1,2,0:T(8,128)S(1)}, u32[]{:S(2)}, u32[]{:S(2)}) collective-permute-start(f32[13,30,1,128]{3,1,2,0:T(8,128)S(1)} %get-tuple-element.24), channel_id=1, source_target_pairs={{0,32},{32,64},{64,96},{96,128},{128,160},{160,192},{192,224},{224... | collective-permute-start | bytes 599048 | tf_op jit(solution)/shard_map/ppermute | solution.py:22
  106.2 8.4 %collective-permute-start.5 = (f32[13,30,1,128]{3,1,2,0:T(8,128)S(1)}, f32[13,30,1,128]{3,1,2,0:T(8,128)S(1)}, u32[]{:S(2)}, u32[]{:S(2)}) collective-permute-start(f32[13,30,1,128]{3,1,2,0:T(8,128)S(1)} %get-tuple-element.25), channel_id=1, source_target_pairs={{32,0},{64,32},{96,64},{128,96},{160,128},{192,160},{224,192},{256... | collective-permute-start | bytes 599048 | tf_op jit(solution)/shard_map/ppermute | solution.py:23
  150.4 9.0 %collective-permute-start.6 = (f32[13,30,1,128]{3,1,2,0:T(8,128)S(1)}, f32[13,30,1,128]{3,1,2,0:T(8,128)S(1)}, u32[]{:S(2)}, u32[]{:S(2)}) collective-permute-start(f32[13,30,1,128]{3,1,2,0:T(8,128)S(1)} %get-tuple-element.20), channel_id=1, source_target_pairs={{0,32},{32,64},{64,96},{96,128},{128,160},{160,192},{192,224},{224... | collective-permute-start | bytes 599048 | tf_op jit(solution)/shard_map/ppermute | solution.py:22
  154.8 8.4 %collective-permute-start.7 = (f32[13,30,1,128]{3,1,2,0:T(8,128)S(1)}, f32[13,30,1,128]{3,1,2,0:T(8,128)S(1)}, u32[]{:S(2)}, u32[]{:S(2)}) collective-permute-start(f32[13,30,1,128]{3,1,2,0:T(8,128)S(1)} %get-tuple-element.21), channel_id=1, source_target_pairs={{32,0},{64,32},{96,64},{128,96},{160,128},{192,160},{224,192},{256... | collective-permute-start | bytes 599048 | tf_op jit(solution)/shard_map/ppermute | solution.py:23
